TPU v7x, 512 devices: a whole 4x8x8 slice. The times are simulated.
512 devices in a mesh: lon: 32 (over y, x), tm: 16 (over z, core).
Axes of the slice: x: 4, y: 8, z: 8, core: 2. Of those that a mesh axis runs over, the one named last changes fastest.
Arguments:
- anomalies: bfloat16 [4096, 8192], P('lon', 'tm'), may hold values from -200 to 200, as said below
- neighbor_ids: int32 [16, 3], replicated, may hold values from 0 to 15, as said below
- neighbor_counts: int32 [16], replicated, may hold values from 1 to 3
- lag_set: int32 [9], replicated, may hold values from 0 to 128, as said below
Outputs:
- network: float32 [4096, 6912], P(('lon', 'tm'))
Inputs may be any that keep to these rules, and one draw needn't show every extreme that they name: `neighbor_ids`: row b lists 3 distinct blocks, each within loop distance 2 of block b (b itself may appear); only the first neighbor_counts[b] slots are used. `lag_set`: 9 distinct lags. Real-valued anomalies; no point's series is constant.
All inputs are finite; a program needn't handle non-finite values.
Results may differ from a plain program's by a relative error of at most 0.0037.
Values may be sent and summed in bfloat16 or wider, within the bound.
No kernel may reach another device: no remote copies, remote signals or barrier semaphores. Data moves between devices by JAX's collectives and lax.ppermute only.
A program may use at most 64 MiB of HBM per device.

v0:
```python
import jax
import jax.numpy as jnp
from jax import lax
from jax.sharding import PartitionSpec as P

LMAX = 128
NLAG = 9
K_SLOTS = 3
REACH = 2


def joined(part, axis, combine):
    gathered = jax.tree.map(lambda a: lax.all_gather(a, axis), part)

    def take(source):
        return jax.tree.map(lambda a: lax.dynamic_index_in_dim(a, source, 0, False), gathered)

    return lax.fori_loop(
        1, lax.axis_size(axis), lambda source, state: combine(state, take(source)), take(0)
    )


def shifted(value, axis, by):
    size = lax.axis_size(axis)
    pairs = [(i, i + by) for i in range(size) if 0 <= i + by < size]
    return lax.ppermute(value, axis, pairs)


def from_partner(value, axis, stride):
    mask = 2**stride
    pairs = [(source, source ^ mask) for source in range(lax.axis_size(axis))]
    return lax.ppermute(value, axis, pairs)


def shifted_2(value, axis, by):
    size = lax.axis_size(axis)
    return lax.ppermute(value, axis, [(i, (i + by) % size) for i in range(size)])


def chan_merge(earlier, later):
    count_first, mean_first, square_first = earlier
    count_second, mean_second, square_second = later
    merged = count_first + count_second
    delta = mean_second - mean_first
    new_mean = mean_first + delta * (count_second / merged)
    new_square = (
        square_first + square_second + delta * delta * (count_first * count_second / merged)
    )
    return (merged, new_mean, new_square)


def left_operand(own_rows, lag_days, days_dev):
    return jnp.concatenate(
        [own_rows[:, :days_dev], lax.dynamic_slice_in_dim(own_rows, lag_days, days_dev, 1)], 1
    )


def right_product(left_side, columns, lag_days, days_dev):
    right_side = jnp.concatenate(
        [lax.dynamic_slice_in_dim(columns, lag_days, days_dev, 1), columns[:, :days_dev]], 1
    )
    return lax.dot_general(
        left_side, right_side, (((1,), (1,)), ((), ())), preferred_element_type=jnp.float32
    )


def local(anomalies, neighbor_ids, neighbor_counts, lag_set):
    half_rows, days_dev = anomalies.shape
    tm_size = lax.axis_size("tm")
    blocks = lax.axis_size("lon") // 2
    block_width = 2 * half_rows
    total_days = days_dev * tm_size
    values = anomalies.astype(jnp.float32)
    shard_mean = jnp.mean(values, axis=1)
    shard_square = jnp.sum(jnp.square(values - shard_mean[:, None]), axis=1)
    shard_count = jnp.full((1,), days_dev, jnp.float32)
    merged_count, point_mean, point_m2 = joined(
        (shard_count, shard_mean, shard_square), "tm", chan_merge
    )
    spread = jnp.sqrt(point_m2 / merged_count + 1e-06)
    standardized = ((values - point_mean[:, None]) / spread[:, None]).astype(jnp.bfloat16)
    margin = shifted(standardized[:, :LMAX], "tm", -1)
    extended = jnp.concatenate([standardized, margin], 1)
    partner = from_partner(extended, "lon", 0)
    lon_index = lax.axis_index("lon")
    parity = lon_index % 2
    own_block = jnp.where(
        parity == 0,
        jnp.concatenate([extended, partner], 0),
        jnp.concatenate([partner, extended], 0),
    )
    block_index = lon_index // 2
    later_blocks = []
    earlier_blocks = []
    for offset in range(1, REACH + 1):
        later_blocks.append(shifted_2(own_block, "lon", -2 * offset))
        earlier_blocks.append(shifted_2(own_block, "lon", 2 * offset))
    candidates = jnp.stack(earlier_blocks[::-1] + [own_block] + later_blocks, 0)
    block_ids = lax.dynamic_index_in_dim(neighbor_ids, block_index, 0, keepdims=False)
    live_count = lax.dynamic_index_in_dim(neighbor_counts, block_index, 0, keepdims=False)
    positions = (block_ids - block_index + REACH) % blocks

    def term_rows(row_count):
        slot_columns = [
            lax.dynamic_index_in_dim(candidates, positions[slot_index], 0, keepdims=False)
            for slot_index in range(K_SLOTS)
        ]
        by_slot = [[] for slot_index in range(K_SLOTS)]
        for lag_index in range(NLAG):
            left_side = left_operand(extended, lag_set[lag_index], days_dev)
            for slot_index in range(K_SLOTS):
                by_slot[slot_index].append(
                    right_product(left_side, slot_columns[slot_index], lag_set[lag_index], days_dev)
                )
        products = [item for slot_list in by_slot for item in slot_list]
        return jnp.stack(products, 1).reshape(row_count, -1)

    out_rows = half_rows // tm_size
    summed = lax.psum(term_rows(half_rows), "tm")
    comoment = lax.dynamic_slice_in_dim(summed, lax.axis_index("tm") * out_rows, out_rows, 0)
    comoment = comoment.reshape(out_rows, K_SLOTS, NLAG, block_width)
    denominator = 2.0 * (total_days - lag_set).astype(jnp.float32)
    is_live = jnp.arange(K_SLOTS, dtype=jnp.int32) < live_count
    linked = jnp.where(
        is_live[None, :, None, None], comoment / denominator[None, None, :, None], 0.0
    )
    squares = jnp.sum(jnp.square(linked), axis=(1, 2, 3))
    row_scale = jnp.sqrt(squares / (live_count * NLAG * block_width).astype(jnp.float32) + 1e-06)
    return (linked / row_scale[:, None, None, None]).reshape(out_rows, -1)


def solution(mesh):
    return jax.shard_map(
        local,
        mesh=mesh,
        in_specs=(P("lon", "tm"), P(), P(), P()),
        out_specs=P(("lon", "tm"), None),
        check_vma=False,
    )
```

profile of v0, /device:TPU:1, one launch (start us, length us, event | category | flops | bytes accessed | tf_op | source)
XLA Modules:
  0.0 342.7 jit_solution(14211399032186157105)
XLA Ops:
  6.5 1.3 dynamic-slice.54
  8.6 30.6 %all-reduce = f32[16]{0:T(128)S(1)} all-reduce(f32[16]{0:T(128)S(1)} %dynamic-update-slice), channel_id=1, replica_groups=mesh['lon'=32,'tm'=16] {'tm'}, use_global_device_ids=true, to_apply=%add | all-reduce | flops 16 | bytes 128
  40.2 1.1 fusion.61
  41.3 16.8 %all-gather.3 = f32[16,1,128]{2,1,0:T(1,128)S(1)} all-gather(f32[1,1,128]{2,1,0:T(1,128)S(1)} %bitcast.237), channel_id=3, replica_groups=mesh['lon'=32,'tm'=16] {'tm'}, dimensions={0}, use_global_device_ids=true | all-gather | bytes 8704 | tf_op jit(solution)/shard_map/all_gather | solution.py:13
  58.1 16.0 %all-gather.2 = f32[16,1,128]{2,1,0:T(1,128)S(1)} all-gather(f32[1,1,128]{2,1,0:T(1,128)S(1)} %get-tuple-element.256), channel_id=2, replica_groups=mesh['lon'=32,'tm'=16] {'tm'}, dimensions={0}, use_global_device_ids=true | all-gather | bytes 8704 | tf_op jit(solution)/shard_map/all_gather | solution.py:13
  74.1 39.3 %while.19 = (s32[]{:T(128)}, f32[1]{0:T(128)}, f32[128]{0:T(128)S(1)}, f32[128]{0:T(128)S(1)}, f32[16,1]{0,1:T(1,128)S(1)}, /*index=5*/f32[16,128]{1,0:T(8,128)S...) while((s32[]{:T(128)}, f32[1]{0:T(128)}, f32[128]{0:T(128)S(1)}, f32[128]{0:T(128)S(1)}, ...), condition=%wide.region_3.4_spmd, body=%wide.region_2.3_spmd.sunk | while | flops 905 | bytes 3295 | solution.py:18
  113.4 1.0 fusion.63
  114.4 2.1 collective-permute-start
  117.4 2.2 collective-permute-done
  119.7 3.1 collective-permute-start.1
  127.3 3.2 collective-permute-start.2
  130.5 1.7 fusion.107
  151.5 4.4 %collective-permute-start.3 = (bf16[256,640]{1,0:T(8,128)(2,1)S(1)}, bf16[256,640]{1,0:T(8,128)(2,1)S(1)}, u32[]{:S(2)}, u32[]{:S(2)}) collective-permute-start(bf16[256,640]{1,0:T(8,128)(2,1)S(1)} %maximum_select_fusion), channel_id=1, source_target_pairs={{0,32},{16,48},{32,64},{48,80},{64,96},{80,112},{96,128},{112,144}... | collective-permute-start | bytes 983048 | tf_op jit(solution)/shard_map/ppermute | solution.py:37
  156.2 4.5 %collective-permute-start.4 = (bf16[256,640]{1,0:T(8,128)(2,1)S(1)}, bf16[256,640]{1,0:T(8,128)(2,1)S(1)}, u32[]{:S(2)}, u32[]{:S(2)}) collective-permute-start(bf16[256,640]{1,0:T(8,128)(2,1)S(1)} %maximum_select_fusion), channel_id=1, source_target_pairs={{0,480},{16,496},{32,0},{48,16},{64,32},{80,48},{96,64},{112,80},{... | collective-permute-start | bytes 983048 | tf_op jit(solution)/shard_map/ppermute | solution.py:37
  160.7 2.8 collective-permute-start.5
  163.6 5.9 %collective-permute-done.3 = bf16[256,640]{1,0:T(8,128)(2,1)S(1)} collective-permute-done((bf16[256,640]{1,0:T(8,128)(2,1)S(1)}, bf16[256,640]{1,0:T(8,128)(2,1)S(1)}, u32[]{:S(2)}, u32[]{:S(2)}) %collective-permute-start.3) | collective-permute-done | bytes 327712 | tf_op jit(solution)/shard_map/ppermute | solution.py:37
  169.6 3.2 collective-permute-done.4
  172.8 2.4 collective-permute-done.5
  175.4 4.5 %dynamic-slice_bitcast_fusion.3 = (bf16[256,512]{1,0:T(8,128)(2,1)S(1)}, bf16[256,512]{1,0:T(8,128)(2,1)S(1)}, bf16[256,512]{1,0:T(8,128)(2,1)S(1)}, bf16[256,51...) fusion(bf16[5,256,640]{2,1,0:T(8,128)(2,1)S(1)} %bitcast_dynami, ...), kind=kLoop, calls=%fused_computation.153 | loop fusion | bytes 14155824 | tf_op jit(solution)/shard_map/dynamic_slice | solution.py:60
  205.8 3.3 copy.9
  209.1 3.0 copy.10
  214.8 118.2 %all-reduce.3.cloned.1.call-done = f32[128,6912]{1,0:T(8,128)} async-done(((f32[128,6912]{1,0:T(8,128)}), f32[128,6912]{1,0:T(8,128)}) %all-reduce.3.cloned.1.call-update) | async-done | bytes 3538960 | tf_op jit(solution)/shard_map/psum | solution.py:119
  333.0 1.1 multiply_reduce_fusion
  334.2 1.7 broadcast_divide_fusion
  (97 shorter events, 41.8 us)
Async XLA Ops:
  6.5 326.5 %all-reduce.3.cloned.1.call-start = ((), (), s32[]{:S(2)}) async-start(), calls=%async_computation | async-start | bytes 7077888 | tf_op jit(solution)/shard_map/psum | solution.py:119
  114.4 5.2 %collective-permute-start = (bf16[128,128]{1,0:T(8,128)(2,1)S(1)}, bf16[128,128]{1,0:T(8,128)(2,1)S(1)}, u32[]{:S(2)}, u32[]{:S(2)}) collective-permute-start(bf16[128,128]{1,0:T(8,128)(2,1)S(1)} %slice.58), channel_id=1, source_target_pairs={{1,0},{2,1},{3,2},{4,3},{5,4},{6,5},{7,6},{8,7},{9,8},{10,9},{11,1... | collective-permute-start | bytes 98312 | tf_op jit(solution)/shard_map/ppermute | solution.py:26
  119.7 7.5 %collective-permute-start.1 = (bf16[128,640]{1,0:T(8,128)(2,1)S(1)}, bf16[128,640]{1,0:T(8,128)(2,1)S(1)}, u32[]{:S(2)}, u32[]{:S(2)}) collective-permute-start(bf16[128,640]{1,0:T(8,128)(2,1)S(1)} %get-tuple-element.242), channel_id=1, source_target_pairs={{0,16},{16,0},{32,48},{48,32},{64,80},{80,64},{96,112},{112,96},{1... | collective-permute-start | bytes 491528 | tf_op jit(solution)/shard_map/ppermute | solution.py:32
  127.3 36.2 %collective-permute-start.2 = (bf16[256,640]{1,0:T(8,128)(2,1)S(1)}, bf16[256,640]{1,0:T(8,128)(2,1)S(1)}, u32[]{:S(2)}, u32[]{:S(2)}) collective-permute-start(bf16[256,640]{1,0:T(8,128)(2,1)S(1)} %maximum_select_fusion), channel_id=1, source_target_pairs={{0,64},{16,80},{32,96},{48,112},{64,128},{80,144},{96,160},{112,17... | collective-permute-start | bytes 983048 | tf_op jit(solution)/shard_map/ppermute | solution.py:37
  151.5 18.0 %collective-permute-start.3 = (bf16[256,640]{1,0:T(8,128)(2,1)S(1)}, bf16[256,640]{1,0:T(8,128)(2,1)S(1)}, u32[]{:S(2)}, u32[]{:S(2)}) collective-permute-start(bf16[256,640]{1,0:T(8,128)(2,1)S(1)} %maximum_select_fusion), channel_id=1, source_target_pairs={{0,32},{16,48},{32,64},{48,80},{64,96},{80,112},{96,128},{112,144}... | collective-permute-start | bytes 983048 | tf_op jit(solution)/shard_map/ppermute | solution.py:37
  156.2 16.6 %collective-permute-start.4 = (bf16[256,640]{1,0:T(8,128)(2,1)S(1)}, bf16[256,640]{1,0:T(8,128)(2,1)S(1)}, u32[]{:S(2)}, u32[]{:S(2)}) collective-permute-start(bf16[256,640]{1,0:T(8,128)(2,1)S(1)} %maximum_select_fusion), channel_id=1, source_target_pairs={{0,480},{16,496},{32,0},{48,16},{64,32},{80,48},{96,64},{112,80},{... | collective-permute-start | bytes 983048 | tf_op jit(solution)/shard_map/ppermute | solution.py:37
  160.7 14.5 %collective-permute-start.5 = (bf16[256,640]{1,0:T(8,128)(2,1)S(1)}, bf16[256,640]{1,0:T(8,128)(2,1)S(1)}, u32[]{:S(2)}, u32[]{:S(2)}) collective-permute-start(bf16[256,640]{1,0:T(8,128)(2,1)S(1)} %maximum_select_fusion), channel_id=1, source_target_pairs={{0,448},{16,464},{32,480},{48,496},{64,0},{80,16},{96,32},{112,48}... | collective-permute-start | bytes 983048 | tf_op jit(solution)/shard_map/ppermute | solution.py:37
  212.1 0.7 copy-start.1
  212.1 2.0 copy-start
Sparse Core Ops, SparseCore 0:
  212.2 120.7 all-reduce.2
where the time goes:
time: 344 us; the launch traced here: 343 us
  waiting for transfers between devices  132 us (38%)
  blocking collectives  63.3 us (18%)
  between operations  36.7 us (11%)
  loops' own time  30.2 us (9%)
  matrix products  25.8 us (8%)
  local copies, waits for them, and re-layouts  25.6 us (7%)
  starting transfers between devices  20.1 us (6%)
  other arithmetic  9.1 us (3%)
    psum x1, waiting for transfers between devices, local(): summed = lax.psum(term_rows(half_rows), 'tm')  118 us
    all_gather x2, blocking collectives, joined(): gathered = jax.tree.map(lambda a: lax.all_gather(a, axis), part)  32.7 us
    unnamed x1, blocking collectives  30.6 us
    another operation x1, loops' own time, joined(): lax.fori_loop(1, lax.axis_size(axis), lambda source, state: combine(state...  30.2 us
    dot_general x27, matrix products, right_product(): lax.dot_general(left_side, right_side, (((1,), (1,)), ((), ())), preferre...  25.8 us
    ppermute x4, starting transfers between devices, shifted_2(): lax.ppermute(value, axis, [(i, (i + by) % size) for i in range(size)])  14.9 us
    ppermute x4, waiting for transfers between devices, shifted_2(): lax.ppermute(value, axis, [(i, (i + by) % size) for i in range(size)])  11.5 us
    dynamic_slice x17, local copies, waits for them, and re-layouts, take(): lax.dynamic_index_in_dim(a, source, 0, False)  8.78 us
  transfers between devices with their start and end apart: 7, of which 5 were waited for; matrix products, arithmetic and copies ran while one was open for 2% of the time, Pallas kernels for 0%

commit v1 on v0

--- a/solution.py
+++ b/solution.py
@@ -116,7 +116,7 @@
         return jnp.stack(products, 1).reshape(row_count, -1)
 
     out_rows = half_rows // tm_size
-    summed = lax.psum(term_rows(half_rows), "tm")
+    summed = jnp.sum(lax.all_gather(term_rows(half_rows), "tm"), axis=0)
     comoment = lax.dynamic_slice_in_dim(summed, lax.axis_index("tm") * out_rows, out_rows, 0)
     comoment = comoment.reshape(out_rows, K_SLOTS, NLAG, block_width)
     denominator = 2.0 * (total_days - lag_set).astype(jnp.float32)

time: 344 us -> 524 us (1.52)
  waiting for transfers between devices: 132 us -> 293 us
  other arithmetic: 9.1 us -> 26.9 us
    all_gather x0 -> x1, waiting for transfers between devices: none -> 279 us  [local(): summed = jnp.sum(lax.all_gather(term_rows(half_rows), 'tm'), axis=0)]
    psum x1 -> x0, waiting for transfers between devices: 118 us -> none  [local(): summed = lax.psum(term_rows(half_rows), 'tm')]
    reduce_sum x0 -> x1, other arithmetic: none -> 18.2 us  [local(): summed = jnp.sum(lax.all_gather(term_rows(half_rows), 'tm'), axis=0)]
  transfers between devices with their start and end apart: 7 -> 7, of which waited for: 5 -> 5; matrix products, arithmetic and copies ran while one was open for 2% -> 1% of each run, Pallas kernels for 0% -> 0%
where the time goes in v1:
time: 524 us; the launch traced here: 522 us
  waiting for transfers between devices  293 us (56%)
  blocking collectives  63.3 us (12%)
  between operations  36.7 us (7%)
  loops' own time  30.2 us (6%)
  other arithmetic  26.9 us (5%)
  local copies, waits for them, and re-layouts  26.2 us (5%)
  matrix products  25.8 us (5%)
  starting transfers between devices  20.1 us (4%)
    all_gather x1, waiting for transfers between devices, local(): summed = jnp.sum(lax.all_gather(term_rows(half_rows), 'tm'), axis=0)  279 us
    all_gather x2, blocking collectives, joined(): gathered = jax.tree.map(lambda a: lax.all_gather(a, axis), part)  32.7 us
    unnamed x1, blocking collectives  30.6 us
    another operation x1, loops' own time, joined(): lax.fori_loop(1, lax.axis_size(axis), lambda source, state: combine(state...  30.2 us
    dot_general x27, matrix products, right_product(): lax.dot_general(left_side, right_side, (((1,), (1,)), ((), ())), preferre...  25.8 us
    reduce_sum x1, other arithmetic, local(): summed = jnp.sum(lax.all_gather(term_rows(half_rows), 'tm'), axis=0)  18.2 us
    ppermute x4, starting transfers between devices, shifted_2(): lax.ppermute(value, axis, [(i, (i + by) % size) for i in range(size)])  14.9 us
    ppermute x4, waiting for transfers between devices, shifted_2(): lax.ppermute(value, axis, [(i, (i + by) % size) for i in range(size)])  11.5 us
  transfers between devices with their start and end apart: 7, of which 5 were waited for; matrix products, arithmetic and copies ran while one was open for 1% of the time, Pallas kernels for 0%

profile of v1, /device:TPU:1, one launch (start us, length us, event | category | flops | bytes accessed | tf_op | source)
XLA Modules:
  0.0 522.3 jit_solution(4495334665383964731)
XLA Ops:
  6.5 1.3 dynamic-slice.54
  8.6 30.6 %all-reduce = f32[16]{0:T(128)S(1)} all-reduce(f32[16]{0:T(128)S(1)} %dynamic-update-slice), channel_id=1, replica_groups=mesh['lon'=32,'tm'=16] {'tm'}, use_global_device_ids=true, to_apply=%add | all-reduce | flops 16 | bytes 128
  40.2 1.1 fusion.61
  41.3 16.8 %all-gather.3 = f32[16,1,128]{2,1,0:T(1,128)S(1)} all-gather(f32[1,1,128]{2,1,0:T(1,128)S(1)} %bitcast.237), channel_id=3, replica_groups=mesh['lon'=32,'tm'=16] {'tm'}, dimensions={0}, use_global_device_ids=true | all-gather | bytes 8704 | tf_op jit(solution)/shard_map/all_gather | solution.py:13
  58.1 16.0 %all-gather.2 = f32[16,1,128]{2,1,0:T(1,128)S(1)} all-gather(f32[1,1,128]{2,1,0:T(1,128)S(1)} %get-tuple-element.256), channel_id=2, replica_groups=mesh['lon'=32,'tm'=16] {'tm'}, dimensions={0}, use_global_device_ids=true | all-gather | bytes 8704 | tf_op jit(solution)/shard_map/all_gather | solution.py:13
  74.1 39.3 %while.19 = (s32[]{:T(128)}, f32[1]{0:T(128)}, f32[128]{0:T(128)S(1)}, f32[128]{0:T(128)S(1)}, f32[16,1]{0,1:T(1,128)S(1)}, /*index=5*/f32[16,128]{1,0:T(8,128)S...) while((s32[]{:T(128)}, f32[1]{0:T(128)}, f32[128]{0:T(128)S(1)}, f32[128]{0:T(128)S(1)}, ...), condition=%wide.region_3.4_spmd, body=%wide.region_2.3_spmd.sunk | while | flops 905 | bytes 3295 | solution.py:18
  113.4 1.0 fusion.63
  114.4 2.1 collective-permute-start
  117.4 2.2 collective-permute-done
  119.7 3.1 collective-permute-start.1
  127.3 3.2 collective-permute-start.2
  130.5 1.7 fusion.107
  151.5 4.4 collective-permute-start.3
  156.2 4.5 collective-permute-start.4
  160.7 2.8 collective-permute-start.5
  163.6 5.9 %collective-permute-done.3 = bf16[256,640]{1,0:T(8,128)(2,1)S(1)} collective-permute-done((bf16[256,640]{1,0:T(8,128)(2,1)S(1)}, bf16[256,640]{1,0:T(8,128)(2,1)S(1)}, u32[]{:S(2)}, u32[]{:S(2)}) %collective-permute-start.3) | collective-permute-done | bytes 327712 | tf_op jit(solution)/shard_map/ppermute | solution.py:37
  169.6 3.2 collective-permute-done.4
  172.8 2.4 collective-permute-done.5
  175.4 4.5 dynamic-slice_bitcast_fusion.3
  205.8 3.3 copy.10
  209.1 3.0 copy.11
  215.5 279.3 %all-gather.6.cloned.1.call-done = f32[16,128,6912]{2,1,0:T(8,128)} async-done(((f32[1,128,6912]{2,1,0:T(8,128)}), f32[16,128,6912]{2,1,0:T(8,128)}) %all-gather.6.cloned.1.call-update) | async-done | bytes 56623120 | tf_op jit(solution)/shard_map/all_gather | solution.py:119
  494.8 18.2 %reduce_sum.38 = f32[128,6912]{1,0:T(8,128)S(1)} reduce(f32[16,128,6912]{2,1,0:T(8,128)} %all-gather.6.cloned.1.call-done, f32[]{:T(128)} %constant.560.clone.1), dimensions={0}, to_apply=%region_4.5 | reduce | flops 13271040 | bytes 60162052 | tf_op jit(solution)/shard_map/reduce_sum | solution.py:119
  513.9 1.5 broadcast_divide_fusion
  (98 shorter events, 43.3 us)
Async XLA Ops:
  6.5 488.3 %all-gather.6.cloned.1.call-start = ((), (), s32[]{:S(2)}) async-start(), calls=%async_computation | async-start | bytes 60162048 | tf_op jit(solution)/shard_map/all_gather | solution.py:119
  114.4 5.2 %collective-permute-start = (bf16[128,128]{1,0:T(8,128)(2,1)S(1)}, bf16[128,128]{1,0:T(8,128)(2,1)S(1)}, u32[]{:S(2)}, u32[]{:S(2)}) collective-permute-start(bf16[128,128]{1,0:T(8,128)(2,1)S(1)} %slice.58), channel_id=1, source_target_pairs={{1,0},{2,1},{3,2},{4,3},{5,4},{6,5},{7,6},{8,7},{9,8},{10,9},{11,1... | collective-permute-start | bytes 98312 | tf_op jit(solution)/shard_map/ppermute | solution.py:26
  119.7 7.5 %collective-permute-start.1 = (bf16[128,640]{1,0:T(8,128)(2,1)S(1)}, bf16[128,640]{1,0:T(8,128)(2,1)S(1)}, u32[]{:S(2)}, u32[]{:S(2)}) collective-permute-start(bf16[128,640]{1,0:T(8,128)(2,1)S(1)} %get-tuple-element.242), channel_id=1, source_target_pairs={{0,16},{16,0},{32,48},{48,32},{64,80},{80,64},{96,112},{112,96},{1... | collective-permute-start | bytes 491528 | tf_op jit(solution)/shard_map/ppermute | solution.py:32
  127.3 36.2 %collective-permute-start.2 = (bf16[256,640]{1,0:T(8,128)(2,1)S(1)}, bf16[256,640]{1,0:T(8,128)(2,1)S(1)}, u32[]{:S(2)}, u32[]{:S(2)}) collective-permute-start(bf16[256,640]{1,0:T(8,128)(2,1)S(1)} %maximum_select_fusion), channel_id=1, source_target_pairs={{0,64},{16,80},{32,96},{48,112},{64,128},{80,144},{96,160},{112,17... | collective-permute-start | bytes 983048 | tf_op jit(solution)/shard_map/ppermute | solution.py:37
  151.5 18.0 %collective-permute-start.3 = (bf16[256,640]{1,0:T(8,128)(2,1)S(1)}, bf16[256,640]{1,0:T(8,128)(2,1)S(1)}, u32[]{:S(2)}, u32[]{:S(2)}) collective-permute-start(bf16[256,640]{1,0:T(8,128)(2,1)S(1)} %maximum_select_fusion), channel_id=1, source_target_pairs={{0,32},{16,48},{32,64},{48,80},{64,96},{80,112},{96,128},{112,144}... | collective-permute-start | bytes 983048 | tf_op jit(solution)/shard_map/ppermute | solution.py:37
  156.2 16.6 %collective-permute-start.4 = (bf16[256,640]{1,0:T(8,128)(2,1)S(1)}, bf16[256,640]{1,0:T(8,128)(2,1)S(1)}, u32[]{:S(2)}, u32[]{:S(2)}) collective-permute-start(bf16[256,640]{1,0:T(8,128)(2,1)S(1)} %maximum_select_fusion), channel_id=1, source_target_pairs={{0,480},{16,496},{32,0},{48,16},{64,32},{80,48},{96,64},{112,80},{... | collective-permute-start | bytes 983048 | tf_op jit(solution)/shard_map/ppermute | solution.py:37
  160.7 14.5 %collective-permute-start.5 = (bf16[256,640]{1,0:T(8,128)(2,1)S(1)}, bf16[256,640]{1,0:T(8,128)(2,1)S(1)}, u32[]{:S(2)}, u32[]{:S(2)}) collective-permute-start(bf16[256,640]{1,0:T(8,128)(2,1)S(1)} %maximum_select_fusion), channel_id=1, source_target_pairs={{0,448},{16,464},{32,480},{48,496},{64,0},{80,16},{96,32},{112,48}... | collective-permute-start | bytes 983048 | tf_op jit(solution)/shard_map/ppermute | solution.py:37
  212.1 0.7 copy-start.1
  212.1 2.0 copy-start
Sparse Core Ops, SparseCore 0:
  212.3 282.4 all-gather.5
